TPU v7x, 512 devices: a whole 4x4x16 slice. The times are simulated.
512 devices in a mesh: dp: 32 (over z, core), freq: 16 (over x, y).
Axes of the slice: x: 4, y: 4, z: 16, core: 2. Of those that a mesh axis runs over, the one named last changes fastest.
Arguments:
- output_grad: bfloat16 [1024, 384, 1024], P(('dp', 'freq')), may hold values from -6 to 6
- layer_input: bfloat16 [1024, 384, 1024], P(('dp', 'freq')), may hold values from -6 to 6
- counts: int32 [512], P(('dp', 'freq')), may hold values from 0 to 2, as said below
- bin_order: int32 [64], replicated, may hold values from 0 to 1023, as said below
- inverse_factor: bfloat16 [64, 2, 384, 384], P('freq'), may hold values from -0.10306207 to 0.70406207
Outputs:
- input_spectra_grad: bfloat16 [1024, 128, 384], P(('dp', 'freq'))
- tap_grad: float32 [9, 384, 384], P(None, 'dp', 'freq')
Inputs may be any that keep to these rules, and one draw needn't show every extreme that they name: `counts`: slots at or past a shard's count hold no image; some shard has all 2 slots live and some has none. `bin_order`: entries are distinct bins of the 32 x 32 grid; slot j belongs to freq index j // 4.
All inputs are finite; a program needn't handle non-finite values.
Results may differ from a plain program's by a relative error of at most 0.0071.
Values may be sent and summed in bfloat16 or wider, within the bound.
No kernel may reach another device: no remote copies, remote signals or barrier semaphores. Data moves between devices by JAX's collectives and lax.ppermute only.
A program may use at most 64 MiB of HBM per device.

v0:
```python
import math
import jax
import jax.numpy as jnp
from jax import lax
from jax.sharding import Mesh, PartitionSpec as P

GRID = 32


def dft_table(bin_order, grid_side):
    pixel_index = jnp.arange(grid_side * grid_side, dtype=jnp.int32)
    row_pos = pixel_index // grid_side
    col_pos = pixel_index % grid_side
    freq_u = bin_order // grid_side
    freq_v = bin_order % grid_side
    phase_turns = (
        row_pos[:, None] * freq_u[None, :] + col_pos[:, None] * freq_v[None, :]
    ) % grid_side
    phase_angle = phase_turns.astype(jnp.float32) * (2.0 * math.pi / grid_side)
    both_parts = jnp.stack([jnp.cos(phase_angle), -jnp.sin(phase_angle)], axis=2) / grid_side
    return both_parts.reshape(grid_side * grid_side, -1).astype(jnp.bfloat16)


def tap_phases(bin_order, grid_side):
    offsets = jnp.arange(9, dtype=jnp.int32)
    shift_y = offsets // 3 - 1
    shift_x = offsets % 3 - 1
    freq_u = bin_order // grid_side
    freq_v = bin_order % grid_side
    phase_turns = (
        freq_u[:, None] * shift_y[None, :] + freq_v[:, None] * shift_x[None, :]
    ) % grid_side
    phase_angle = phase_turns.astype(jnp.float32) * (2.0 * math.pi / grid_side)
    return (jnp.cos(phase_angle), jnp.sin(phase_angle))


def local(output_grad, layer_input, counts, bin_order, inverse_factor):
    slot_count, channels, pixels = output_grad.shape
    freq_devices = lax.axis_size("freq")
    data_devices = lax.axis_size("z") * lax.axis_size("c")
    bins_local = inverse_factor.shape[0]
    total_bins = bin_order.shape[0]
    live_mask = (jnp.arange(slot_count, dtype=jnp.int32) < counts[0]).astype(jnp.bfloat16)
    bins_table = dft_table(bin_order, GRID)

    def spectrum(images):
        masked = images * live_mask[:, None, None]
        return jnp.einsum(
            "scp,pk->skc", masked, bins_table, preferred_element_type=jnp.float32
        ).astype(jnp.bfloat16)

    both_spec = jnp.stack([spectrum(output_grad), spectrum(layer_input)], axis=0)
    both_recv = lax.all_to_all(both_spec, "freq", split_axis=2, concat_axis=1, tiled=True)
    image_rows = both_recv.shape[1]
    parts = both_recv.reshape(2, image_rows, bins_local, 2, channels)
    grad_real = parts[0, :, :, 0]
    grad_imag = parts[0, :, :, 1]
    input_real = parts[1, :, :, 0]
    input_imag = parts[1, :, :, 1]
    factor_real = inverse_factor[:, 0]
    factor_imag = inverse_factor[:, 1]
    f32 = jnp.float32

    def mm(x, p, eq):
        return jnp.einsum(eq, x, p, preferred_element_type=f32)

    u_real = mm(grad_real, factor_real, "ibr,brc->ibc") + mm(grad_imag, factor_imag, "ibr,brc->ibc")
    u_imag = mm(grad_imag, factor_real, "ibr,brc->ibc") - mm(grad_real, factor_imag, "ibr,brc->ibc")
    back_real = 2.0 * u_real - grad_real.astype(f32)
    back_imag = 2.0 * u_imag - grad_imag.astype(f32)
    back_both = (
        jnp.stack([back_real, back_imag], axis=2)
        .astype(jnp.bfloat16)
        .reshape(image_rows, 2 * bins_local, channels)
    )
    returned = lax.all_to_all(back_both, "freq", split_axis=0, concat_axis=1, tiled=True)
    v_real = mm(input_real, factor_real, "ibk,bck->ibc") - mm(
        input_imag, factor_imag, "ibk,bck->ibc"
    )
    v_imag = mm(input_real, factor_imag, "ibk,bck->ibc") + mm(
        input_imag, factor_real, "ibk,bck->ibc"
    )
    local_bins = lax.dynamic_slice_in_dim(
        bin_order, lax.axis_index("freq") * bins_local, bins_local
    )
    cos_local, sin_local = tap_phases(local_bins, GRID)
    cos_t = cos_local.T[:, None, :, None]
    sin_t = sin_local.T[:, None, :, None]
    ur = u_real[None]
    ui = u_imag[None]
    z_t = jnp.stack([cos_t * ur - sin_t * ui, cos_t * ui + sin_t * ur], axis=1).astype(jnp.bfloat16)
    w_t = jnp.stack([cos_t * ur + sin_t * ui, cos_t * ui - sin_t * ur], axis=1).astype(jnp.bfloat16)
    y_all = jnp.stack([v_real, v_imag], axis=0).astype(jnp.bfloat16)
    taps = z_t.shape[0]
    col_share = channels // freq_devices
    row_share = channels // data_devices
    y_cols = y_all.reshape(2, image_rows, bins_local, freq_devices, col_share)
    w_cols = w_t.reshape(taps, 2, image_rows, bins_local, freq_devices, col_share)
    first = jnp.einsum("teibr,eibfc->ftrc", z_t, y_cols, preferred_element_type=f32)
    second = jnp.einsum("eibr,teibfc->ftrc", y_all, w_cols, preferred_element_type=f32)
    gram_scale = 1.0 / math.sqrt(data_devices * freq_devices * slot_count)
    tap_scale = 2.0 * gram_scale / math.sqrt(total_bins)
    col_pieces = ((second - first) * tap_scale).astype(jnp.bfloat16)
    col_pieces = lax.all_to_all(col_pieces, "freq", split_axis=0, concat_axis=0, tiled=True)
    col_sum = jnp.sum(col_pieces.astype(f32), axis=0)
    z_devices = lax.axis_size("z")
    core_devices = lax.axis_size("c")
    row_pieces = jnp.transpose(
        col_sum.astype(jnp.bfloat16).reshape(taps, z_devices, core_devices, row_share, col_share),
        (2, 1, 0, 3, 4),
    )
    row_pieces = lax.all_to_all(row_pieces, "c", split_axis=0, concat_axis=0, tiled=True)
    row_pieces = jnp.sum(row_pieces.astype(f32), axis=0).astype(jnp.bfloat16)
    row_pieces = lax.all_to_all(row_pieces, "z", split_axis=0, concat_axis=0, tiled=True)
    tap_grad = jnp.sum(row_pieces.astype(f32), axis=0)
    return (returned, tap_grad)


def solution(mesh):
    cores = 2
    chips = Mesh(
        mesh.devices.reshape(mesh.shape["dp"] // cores, cores, mesh.shape["freq"]),
        ("z", "c", "freq"),
    )
    return jax.shard_map(
        local,
        mesh=chips,
        in_specs=(
            P(("z", "c", "freq"), None, None),
            P(("z", "c", "freq"), None, None),
            P(("z", "c", "freq")),
            P(),
            P("freq", None, None, None),
        ),
        out_specs=(P(("z", "c", "freq"), None, None), P(None, ("z", "c"), "freq")),
        check_vma=False,
    )
```

profile of v0, /device:TPU:8, one launch (start us, length us, event | category | flops | bytes accessed | tf_op | source)
XLA Modules:
  0.0 136.7 jit_solution(17668139572337699015)
XLA Ops:
  2.1 1.1 fusion.84
  4.4 2.1 %fusion.40 = bf16[1,2,128,384]{3,2,1,0:T(8,128)(2,1)S(1)} fusion(bf16[1024,128,1]{0,1,2:T(8,128)(2,1)S(1)} %reshape.456, bf16[2,384,1024]{2,1,0:T(8,128)(2,1)} %param.5, bf16[2]{0:T(256)(128)(2,1)S(1)} %compare_convert_fusion), kind=kOutput, calls=%fused_computation.38 | convolution fusion | flops 204570624 | bytes 2031620 | tf_op jit(solution)/shard_map/scp,pk->skc/dot_general | solution.py:48
  6.6 1.2 copy.110
  7.8 9.2 %all-to-all-start = ((bf16[2,2,128,384]{3,1,0,2:T(2,128)(2,1)}), bf16[2,2,128,384]{3,1,0,2:T(2,128)(2,1)S(1)}, u32[]{:S(2)}, u32[]{:S(2)}) async-start(bf16[2,2,128,384]{3,1,0,2:T(2,128)(2,1)} %copy.110), calls=%async_computation | async-start | bytes 786432 | tf_op jit(solution)/shard_map/all_to_all | solution.py:53
  17.2 7.4 %all-to-all-done = bf16[2,2,128,384]{3,1,0,2:T(2,128)(2,1)S(1)} async-done(((bf16[2,2,128,384]{3,1,0,2:T(2,128)(2,1)}), bf16[2,2,128,384]{3,1,0,2:T(2,128)(2,1)S(1)}, u32[]{:S(2)}, u32[]{:S(2)}) %all-to-all-start) | async-done | bytes 393248 | tf_op jit(solution)/shard_map/all_to_all | solution.py:53
  29.2 1.3 copy.124
  31.2 1.3 copy.125
  35.4 2.0 %add_convert_fusion = (bf16[9,1,32,4,16,24]{2,5,1,3,4,0:T(8,128)(2,1)S(1)}, bf16[9,1,32,4,16,24]{2,5,1,3,4,0:T(8,128)(2,1)S(1)}) fusion(f32[32,4,16,24]{0,3,1,2:T(8,128)S(1)} %copy.120, f32[9,4]{1,0:T(8,128)S(1)} %get-tuple-element.21, f32[32,4,16,24]{0,3,1,2:T(8,128)S(1)} %copy.119, f32[9,4]{1,0:T(8,128)S(1)} %get-tuple-element.20), kind=kLoop, calls=%fused_computation.5 | loop fusion | flops 3538944 | bytes 2162976 | tf_op jit(solution)/shard_map/convert.12
  37.5 1.1 fusion.8
  38.6 4.4 %fusion.5 = bf16[16,9,384,24]{2,3,0,1:T(8,128)(2,1)S(1)} fusion(f32[16,24,9,384,1,1]{3,1,5,4,0,2:T(8,128)S(1)} %fusion.8, bf16[9,1,32,4,16,24]{2,5,1,3,4,0:T(8,128)(2,1)S(1)} %get-tuple-element.11, bf16[9,1,32,4,16,24]{2,5,1,3,4,0:T(8,128)(2,1)S(1)} %get-tuple-element.10, bf16[1,32,4,384]{3,1,2,0:T(8,128)(2,1)S(1)} %bitcast.148, ...), kind=kOutput, calls=%fused_computation.8 | convolution fusion | flops 684441600 | bytes 9928704 | tf_op jit(solution)/shard_map/eibr,teibfc->ftrc/dot_general | solution.py:100
  43.0 1.8 %copy.126 = bf16[16,9,384,24]{2,3,1,0:T(8,128)(2,1)} copy(bf16[16,9,384,24]{2,3,0,1:T(8,128)(2,1)S(1)} %fusion.5) | data formatting | bytes 5308416 | tf_op jit(solution)/shard_map/convert_element_type | solution.py:103
  44.8 5.3 %all-to-all-start.2 = ((bf16[16,9,384,24]{2,3,1,0:T(8,128)(2,1)}), bf16[16,9,384,24]{2,3,1,0:T(8,128)(2,1)S(1)}, u32[]{:S(2)}, u32[]{:S(2)}) async-start(bf16[16,9,384,24]{2,3,1,0:T(8,128)(2,1)} %copy.126), calls=%async_computation.2 | async-start | bytes 5308416 | tf_op jit(solution)/shard_map/all_to_all | solution.py:104
  51.0 31.2 %all-to-all-done.2 = bf16[16,9,384,24]{2,3,1,0:T(8,128)(2,1)S(1)} async-done(((bf16[16,9,384,24]{2,3,1,0:T(8,128)(2,1)}), bf16[16,9,384,24]{2,3,1,0:T(8,128)(2,1)S(1)}, u32[]{:S(2)}, u32[]{:S(2)}) %all-to-all-start.2) | async-done | bytes 2654240 | tf_op jit(solution)/shard_map/all_to_all | solution.py:104
  82.6 4.0 %reshape.455 = bf16[9,16,2,12,24]{3,2,1,4,0:T(2,128)(2,1)S(1)} reshape(bf16[9,384,24]{1,2,0:T(8,128)(2,1)S(1)} %reduce_sum.33) | data formatting | bytes 331776 | tf_op jit(solution)/shard_map/reshape | solution.py:109
  86.6 2.6 %copy.127 = bf16[2,16,9,12,24]{4,1,3,2,0:T(8,128)(2,1)S(1)} copy(bf16[2,16,9,12,24]{3,0,1,4,2:T(2,128)(2,1)S(1)} %bitcast.139) | data formatting | bytes 331776 | tf_op jit(solution)/shard_map/transpose | solution.py:108
  89.3 1.2 reshape.463
  90.4 3.8 %all_to_all.48 = bf16[2,2,20736]{2,1,0:T(2,128)(2,1)S(1)} all-to-all(bf16[2,2,20736]{2,1,0:T(2,128)(2,1)S(1)} %reshape.463), channel_id=1, replica_groups=mesh['z'=16,'c'=2,'freq'=16] {'c'}, dimensions={0} | all-to-all | bytes 331776 | tf_op jit(solution)/shard_map/all_to_all | solution.py:112
  94.3 6.0 %all-to-all-start.1 = ((bf16[32,8,384]{2,1,0:T(8,128)(2,1)}), bf16[32,8,384]{2,1,0:T(8,128)(2,1)S(1)}, u32[]{:S(2)}, u32[]{:S(2)}) async-start(bf16[32,8,384]{2,1,0:T(8,128)(2,1)} %copy.117), calls=%async_computation.1 | async-start | bytes 393216 | tf_op jit(solution)/shard_map/all_to_all | solution.py:76
  100.3 1.2 reshape.464
  101.9 1.2 reshape.465
  103.1 4.0 %all-to-all-done.1 = bf16[32,8,384]{2,1,0:T(8,128)(2,1)S(1)} async-done(((bf16[32,8,384]{2,1,0:T(8,128)(2,1)}), bf16[32,8,384]{2,1,0:T(8,128)(2,1)S(1)}, u32[]{:S(2)}, u32[]{:S(2)}) %all-to-all-start.1) | async-done | bytes 196640 | tf_op jit(solution)/shard_map/all_to_all | solution.py:76
  107.1 15.2 %all-to-all-start.4 = ((bf16[16,2,1296]{2,1,0:T(2,128)(2,1)}), bf16[16,2,1296]{2,1,0:T(2,128)(2,1)S(1)}, u32[]{:S(2)}, u32[]{:S(2)}) async-start(bf16[16,2,1296]{2,1,0:T(2,128)(2,1)} %reshape.465), calls=%async_computation.4 | async-start | bytes 180224 | tf_op jit(solution)/shard_map/all_to_all | solution.py:114
  123.0 12.2 %all-to-all-done.4 = bf16[16,2,1296]{2,1,0:T(2,128)(2,1)S(1)} async-done(((bf16[16,2,1296]{2,1,0:T(2,128)(2,1)}), bf16[16,2,1296]{2,1,0:T(2,128)(2,1)S(1)}, u32[]{:S(2)}, u32[]{:S(2)}) %all-to-all-start.4) | async-done | bytes 82976 | tf_op jit(solution)/shard_map/all_to_all | solution.py:114
  135.9 0.9 convert_reduce_fusion
  (53 shorter events, 13.2 us)
Async XLA Ops:
  0.6 3.0 %copy-start.6 = (bf16[2,384,1024]{2,1,0:T(8,128)(2,1)S(1)}, bf16[2,384,1024]{2,1,0:T(8,128)(2,1)}, u32[]{:S(2)}) copy-start(bf16[2,384,1024]{2,1,0:T(8,128)(2,1)} %param.6) | copy-start | bytes 4718596
  4.4 12.5 %copy-start.5 = (s32[64]{0:T(128)S(1)}, s32[64]{0:T(128)}, u32[]{:S(2)}) copy-start(s32[64]{0:T(128)} %param.8) | copy-start | bytes 772
  6.6 18.9 %copy-start = (bf16[4,2,384,384]{3,2,1,0:T(8,128)(2,1)S(1)}, bf16[4,2,384,384]{3,2,1,0:T(8,128)(2,1)}, u32[]{:S(2)}) copy-start(bf16[4,2,384,384]{3,2,1,0:T(8,128)(2,1)} %param.9) | copy-start | bytes 7077892
  7.8 16.8 %all-to-all-start = ((bf16[2,2,128,384]{3,1,0,2:T(2,128)(2,1)}), bf16[2,2,128,384]{3,1,0,2:T(2,128)(2,1)S(1)}, u32[]{:S(2)}, u32[]{:S(2)}) async-start(bf16[2,2,128,384]{3,1,0,2:T(2,128)(2,1)} %copy.110), calls=%async_computation | async-start | bytes 786432 | tf_op jit(solution)/shard_map/all_to_all | solution.py:53
  27.3 3.2 %copy-start.3 = (bf16[4,32,384]{2,1,0:T(8,128)(2,1)}, bf16[4,32,384]{2,1,0:T(8,128)(2,1)S(1)}, u32[]{:S(2)}) copy-start(bf16[4,32,384]{2,1,0:T(8,128)(2,1)S(1)} %fusion.61) | copy-start | bytes 294916
  35.4 2.0 %copy-start.1 = (bf16[1,32,4,16,24]{1,4,0,2,3:T(8,128)(2,1)S(1)}, bf16[1,32,4,16,24]{1,4,0,2,3:T(8,128)(2,1)}, u32[]{:S(2)}) copy-start(bf16[1,32,4,16,24]{1,4,0,2,3:T(8,128)(2,1)} %copy.124) | copy-start | bytes 294916
  35.4 2.0 %copy-start.2 = (bf16[1,32,4,16,24]{1,4,0,2,3:T(8,128)(2,1)S(1)}, bf16[1,32,4,16,24]{1,4,0,2,3:T(8,128)(2,1)}, u32[]{:S(2)}) copy-start(bf16[1,32,4,16,24]{1,4,0,2,3:T(8,128)(2,1)} %copy.125) | copy-start | bytes 294916
  37.5 1.1 copy-start.4
  44.8 37.4 %all-to-all-start.2 = ((bf16[16,9,384,24]{2,3,1,0:T(8,128)(2,1)}), bf16[16,9,384,24]{2,3,1,0:T(8,128)(2,1)S(1)}, u32[]{:S(2)}, u32[]{:S(2)}) async-start(bf16[16,9,384,24]{2,3,1,0:T(8,128)(2,1)} %copy.126), calls=%async_computation.2 | async-start | bytes 5308416 | tf_op jit(solution)/shard_map/all_to_all | solution.py:104
  94.3 12.8 %all-to-all-start.1 = ((bf16[32,8,384]{2,1,0:T(8,128)(2,1)}), bf16[32,8,384]{2,1,0:T(8,128)(2,1)S(1)}, u32[]{:S(2)}, u32[]{:S(2)}) async-start(bf16[32,8,384]{2,1,0:T(8,128)(2,1)} %copy.117), calls=%async_computation.1 | async-start | bytes 393216 | tf_op jit(solution)/shard_map/all_to_all | solution.py:76
  107.1 28.1 %all-to-all-start.4 = ((bf16[16,2,1296]{2,1,0:T(2,128)(2,1)}), bf16[16,2,1296]{2,1,0:T(2,128)(2,1)S(1)}, u32[]{:S(2)}, u32[]{:S(2)}) async-start(bf16[16,2,1296]{2,1,0:T(2,128)(2,1)} %reshape.465), calls=%async_computation.4 | async-start | bytes 180224 | tf_op jit(solution)/shard_map/all_to_all | solution.py:114
where the time goes:
time: 137 us
  waiting for transfers between devices  54.9 us (40%)
  starting transfers between devices  35.7 us (26%)
  local copies, waits for them, and re-layouts  22.8 us (17%)
  matrix products  11.4 us (8%)
  other arithmetic  6.38 us (5%)
  blocking collectives  3.85 us (3%)
  between operations  1.78 us (1%)
    all_to_all x1, waiting for transfers between devices, local(): lax.all_to_all(col_pieces, 'freq', split_axis=0, concat_axis=0, tiled=True)  31.2 us
    all_to_all x1, starting transfers between devices, local(): lax.all_to_all(row_pieces, 'z', split_axis=0, concat_axis=0, tiled=True)  15.2 us
    all_to_all x1, waiting for transfers between devices, local(): lax.all_to_all(row_pieces, 'z', split_axis=0, concat_axis=0, tiled=True)  12.2 us
    all_to_all x1, starting transfers between devices, local(): lax.all_to_all(both_spec, 'freq', split_axis=2, concat_axis=1, tiled=True)  9.16 us
    all_to_all x1, waiting for transfers between devices, local(): lax.all_to_all(both_spec, 'freq', split_axis=2, concat_axis=1, tiled=True)  7.36 us
    all_to_all x1, starting transfers between devices, local(): lax.all_to_all(back_both, 'freq', split_axis=0, concat_axis=1, tiled=True)  6.01 us
    all_to_all x1, starting transfers between devices, local(): lax.all_to_all(col_pieces, 'freq', split_axis=0, concat_axis=0, tiled=True)  5.34 us
    dot_general x1, matrix products, local(): jnp.einsum('eibr,teibfc->ftrc', y_all, w_cols, preferred_element_type=f32)  4.44 us
  transfers between devices with their start and end apart: 4, of which 4 were waited for; matrix products, arithmetic and copies ran while one was open for 3% of the time, Pallas kernels for 0%

commit v1 on v0

--- a/solution.py
+++ b/solution.py
@@ -73,7 +73,19 @@
         .astype(jnp.bfloat16)
         .reshape(image_rows, 2 * bins_local, channels)
     )
-    returned = lax.all_to_all(back_both, "freq", split_axis=0, concat_axis=1, tiled=True)
+    ways, here = (lax.axis_size("freq"), lax.axis_index("freq"))
+    width = back_both.shape[0] // ways
+    shape = list(back_both.shape)
+    shape[0] = width
+    height = shape[1]
+    shape[1] = height * ways
+    full = jnp.zeros(shape, back_both.dtype)
+    for mask in range(ways):
+        part = lax.dynamic_slice_in_dim(back_both, (here ^ mask) * width, width, axis=0)
+        if mask:
+            part = lax.ppermute(part, "freq", [(d, d ^ mask) for d in range(ways)])
+        full = lax.dynamic_update_slice_in_dim(full, part, (here ^ mask) * height, axis=1)
+    returned = full
     v_real = mm(input_real, factor_real, "ibk,bck->ibc") - mm(
         input_imag, factor_imag, "ibk,bck->ibc"
     )

time: 137 us -> 229 us (1.67)
  the two profiles are of different devices: /device:TPU:8 before, /device:TPU:26 now
where the time goes in v1:
time: 229 us; the launch traced here: 228 us
  starting transfers between devices  84.3 us (37%)
  waiting for transfers between devices  80.4 us (35%)
  local copies, waits for them, and re-layouts  29.7 us (13%)
  matrix products  17 us (7%)
  other arithmetic  10.6 us (5%)
  blocking collectives  3.85 us (2%)
  between operations  2.29 us (1%)
    ppermute x15, waiting for transfers between devices, local(): part = lax.ppermute(part, 'freq', [(d, d ^ mask) for d in range(ways)])  62.9 us
    ppermute x15, starting transfers between devices, local(): part = lax.ppermute(part, 'freq', [(d, d ^ mask) for d in range(ways)])  48.9 us
    all_to_all x1, starting transfers between devices, local(): lax.all_to_all(row_pieces, 'z', split_axis=0, concat_axis=0, tiled=True)  17.4 us
    all_to_all x1, waiting for transfers between devices, local(): lax.all_to_all(row_pieces, 'z', split_axis=0, concat_axis=0, tiled=True)  12.2 us
    all_to_all x1, starting transfers between devices, local(): lax.all_to_all(col_pieces, 'freq', split_axis=0, concat_axis=0, tiled=True)  9.04 us
    all_to_all x1, starting transfers between devices, local(): lax.all_to_all(both_spec, 'freq', split_axis=2, concat_axis=1, tiled=True)  8.95 us
    dot_general x8, matrix products, mm(): return jnp.einsum(eq, x, p, preferred_element_type=f32)  8.62 us
    all_to_all x1, waiting for transfers between devices, local(): lax.all_to_all(both_spec, 'freq', split_axis=2, concat_axis=1, tiled=True)  5.23 us
  transfers between devices with their start and end apart: 18, of which 12 were waited for; matrix products, arithmetic and copies ran while one was open for 14% of the time, Pallas kernels for 0%

profile of v1, /device:TPU:26, one launch (start us, length us, event | category | flops | bytes accessed | tf_op | source)
XLA Modules:
  0.0 228.2 jit_solution(9705594292170274228)
XLA Ops:
  7.8 8.9 %all-to-all-start = ((bf16[2,2,128,384]{3,1,0,2:T(2,128)(2,1)}), bf16[2,2,128,384]{3,1,0,2:T(2,128)(2,1)S(1)}, u32[]{:S(2)}, u32[]{:S(2)}) async-start(bf16[2,2,128,384]{3,1,0,2:T(2,128)(2,1)} %copy.152), calls=%async_computation | async-start | bytes 786432 | tf_op jit(solution)/shard_map/all_to_all | solution.py:53
  17.2 5.2 %all-to-all-done = bf16[2,2,128,384]{3,1,0,2:T(2,128)(2,1)S(1)} async-done(((bf16[2,2,128,384]{3,1,0,2:T(2,128)(2,1)}), bf16[2,2,128,384]{3,1,0,2:T(2,128)(2,1)S(1)}, u32[]{:S(2)}, u32[]{:S(2)}) %all-to-all-start) | async-done | bytes 393248 | tf_op jit(solution)/shard_map/all_to_all | solution.py:53
  41.2 4.7 %collective-permute-start.14 = (bf16[2,8,384]{2,0,1:T(2,128)(2,1)S(1)}, bf16[2,8,384]{2,0,1:T(2,128)(2,1)}, u32[]{:S(2)}, u32[]{:S(2)}) collective-permute-start(bf16[2,8,384]{2,0,1:T(2,128)(2,1)S(1)} %get-tuple-element.18), channel_id=1, source_target_pairs={{0,15},{1,14},{2,13},{3,12},{4,11},{5,10},{6,9},{7,8},{8,7},{9,6},... | collective-permute-start | bytes 36872 | tf_op jit(solution)/shard_map/ppermute | solution.py:86
  49.2 3.3 %collective-permute-start.12 = (bf16[2,8,384]{2,0,1:T(2,128)(2,1)}, bf16[2,8,384]{2,0,1:T(2,128)(2,1)}, u32[]{:S(2)}, u32[]{:S(2)}) collective-permute-start(bf16[2,8,384]{2,0,1:T(2,128)(2,1)} %get-tuple-element.20), channel_id=1, source_target_pairs={{0,13},{1,12},{2,15},{3,14},{4,9},{5,8},{6,11},{7,10},{8,5},{9,4},... | collective-permute-start | bytes 36872 | tf_op jit(solution)/shard_map/ppermute | solution.py:86
  68.4 4.4 %fusion.5 = bf16[16,9,384,24]{2,3,0,1:T(8,128)(2,1)S(1)} fusion(f32[16,24,9,384,1,1]{3,1,5,4,0,2:T(8,128)S(1)} %fusion.8, bf16[9,1,32,4,16,24]{2,5,1,3,4,0:T(8,128)(2,1)S(1)} %get-tuple-element.11, bf16[9,1,32,4,16,24]{2,5,1,3,4,0:T(8,128)(2,1)S(1)} %get-tuple-element.10, bf16[1,32,4,384]{3,1,2,0:T(8,128)(2,1)S(1)} %bitcast.141, ...), kind=kOutput, calls=%fused_computation.8 | convolution fusion | flops 684441600 | bytes 9928704 | tf_op jit(solution)/shard_map/eibr,teibfc->ftrc/dot_general | solution.py:112
  74.7 9.0 %all-to-all-start.1 = ((bf16[16,9,384,24]{2,3,1,0:T(8,128)(2,1)}), bf16[16,9,384,24]{2,3,1,0:T(8,128)(2,1)S(1)}, u32[]{:S(2)}, u32[]{:S(2)}) async-start(bf16[16,9,384,24]{2,3,1,0:T(8,128)(2,1)} %copy.182), calls=%async_computation.1 | async-start | bytes 5308416 | tf_op jit(solution)/shard_map/all_to_all | solution.py:116
  83.8 3.4 %collective-permute-start.1 = (bf16[2,8,384]{2,0,1:T(2,128)(2,1)S(1)}, bf16[2,8,384]{2,0,1:T(2,128)(2,1)S(1)}, u32[]{:S(2)}, u32[]{:S(2)}) collective-permute-start(bf16[2,8,384]{2,0,1:T(2,128)(2,1)S(1)} %copy-done.21), channel_id=1, source_target_pairs={{0,2},{1,3},{2,0},{3,1},{4,6},{5,7},{6,4},{7,5},{8,10},{9,11},{10,... | collective-permute-start | bytes 36872 | tf_op jit(solution)/shard_map/ppermute | solution.py:86
  87.9 21.6 %collective-permute-done.1 = bf16[2,8,384]{2,0,1:T(2,128)(2,1)S(1)} collective-permute-done((bf16[2,8,384]{2,0,1:T(2,128)(2,1)S(1)}, bf16[2,8,384]{2,0,1:T(2,128)(2,1)S(1)}, u32[]{:S(2)}, u32[]{:S(2)}) %collective-permute-start.1) | collective-permute-done | bytes 12320 | tf_op jit(solution)/shard_map/ppermute | solution.py:86
  111.5 4.9 %collective-permute-done.2 = bf16[2,8,384]{2,0,1:T(2,128)(2,1)S(1)} collective-permute-done((bf16[2,8,384]{2,0,1:T(2,128)(2,1)S(1)}, bf16[2,8,384]{2,0,1:T(2,128)(2,1)S(1)}, u32[]{:S(2)}, u32[]{:S(2)}) %collective-permute-start.2) | collective-permute-done | bytes 12320 | tf_op jit(solution)/shard_map/ppermute | solution.py:86
  118.3 3.6 %collective-permute-done.3 = bf16[2,8,384]{2,0,1:T(2,128)(2,1)S(1)} collective-permute-done((bf16[2,8,384]{2,0,1:T(2,128)(2,1)S(1)}, bf16[2,8,384]{2,0,1:T(2,128)(2,1)S(1)}, u32[]{:S(2)}, u32[]{:S(2)}) %collective-permute-start.3) | collective-permute-done | bytes 12320 | tf_op jit(solution)/shard_map/ppermute | solution.py:86
  123.8 4.5 %collective-permute-done.4 = bf16[2,8,384]{2,0,1:T(2,128)(2,1)S(1)} collective-permute-done((bf16[2,8,384]{2,0,1:T(2,128)(2,1)S(1)}, bf16[2,8,384]{2,0,1:T(2,128)(2,1)S(1)}, u32[]{:S(2)}, u32[]{:S(2)}) %collective-permute-start.4) | collective-permute-done | bytes 12320 | tf_op jit(solution)/shard_map/ppermute | solution.py:86
  130.3 6.0 %collective-permute-done.5 = bf16[2,8,384]{2,0,1:T(2,128)(2,1)S(1)} collective-permute-done((bf16[2,8,384]{2,0,1:T(2,128)(2,1)S(1)}, bf16[2,8,384]{2,0,1:T(2,128)(2,1)S(1)}, u32[]{:S(2)}, u32[]{:S(2)}) %collective-permute-start.5) | collective-permute-done | bytes 12320 | tf_op jit(solution)/shard_map/ppermute | solution.py:86
  138.3 5.8 %collective-permute-done.6 = bf16[2,8,384]{2,0,1:T(2,128)(2,1)S(1)} collective-permute-done((bf16[2,8,384]{2,0,1:T(2,128)(2,1)S(1)}, bf16[2,8,384]{2,0,1:T(2,128)(2,1)S(1)}, u32[]{:S(2)}, u32[]{:S(2)}) %collective-permute-start.6) | collective-permute-done | bytes 12320 | tf_op jit(solution)/shard_map/ppermute | solution.py:86
  144.1 6.9 %collective-permute-start.7 = (bf16[2,8,384]{2,0,1:T(2,128)(2,1)S(1)}, bf16[2,8,384]{2,0,1:T(2,128)(2,1)S(1)}, u32[]{:S(2)}, u32[]{:S(2)}) collective-permute-start(bf16[2,8,384]{2,0,1:T(2,128)(2,1)S(1)} %copy-done.15), channel_id=1, source_target_pairs={{0,8},{1,9},{2,10},{3,11},{4,12},{5,13},{6,14},{7,15},{8,0},{9,1},... | collective-permute-start | bytes 36872 | tf_op jit(solution)/shard_map/ppermute | solution.py:86
  152.6 3.3 %collective-permute-start.8 = (bf16[2,8,384]{2,0,1:T(2,128)(2,1)S(1)}, bf16[2,8,384]{2,0,1:T(2,128)(2,1)S(1)}, u32[]{:S(2)}, u32[]{:S(2)}) collective-permute-start(bf16[2,8,384]{2,0,1:T(2,128)(2,1)S(1)} %copy-done.14), channel_id=1, source_target_pairs={{0,9},{1,8},{2,11},{3,10},{4,13},{5,12},{6,15},{7,14},{8,1},{9,0},... | collective-permute-start | bytes 36872 | tf_op jit(solution)/shard_map/ppermute | solution.py:86
  156.0 4.6 %collective-permute-done.8 = bf16[2,8,384]{2,0,1:T(2,128)(2,1)S(1)} collective-permute-done((bf16[2,8,384]{2,0,1:T(2,128)(2,1)S(1)}, bf16[2,8,384]{2,0,1:T(2,128)(2,1)S(1)}, u32[]{:S(2)}, u32[]{:S(2)}) %collective-permute-start.8) | collective-permute-done | bytes 12320 | tf_op jit(solution)/shard_map/ppermute | solution.py:86
  160.6 3.4 %collective-permute-start.9 = (bf16[2,8,384]{2,0,1:T(2,128)(2,1)S(1)}, bf16[2,8,384]{2,0,1:T(2,128)(2,1)S(1)}, u32[]{:S(2)}, u32[]{:S(2)}) collective-permute-start(bf16[2,8,384]{2,0,1:T(2,128)(2,1)S(1)} %copy-done.13), channel_id=1, source_target_pairs={{0,10},{1,11},{2,8},{3,9},{4,14},{5,15},{6,12},{7,13},{8,2},{9,3},... | collective-permute-start | bytes 36872 | tf_op jit(solution)/shard_map/ppermute | solution.py:86
  164.0 6.1 %collective-permute-done.9 = bf16[2,8,384]{2,0,1:T(2,128)(2,1)S(1)} collective-permute-done((bf16[2,8,384]{2,0,1:T(2,128)(2,1)S(1)}, bf16[2,8,384]{2,0,1:T(2,128)(2,1)S(1)}, u32[]{:S(2)}, u32[]{:S(2)}) %collective-permute-start.9) | collective-permute-done | bytes 12320 | tf_op jit(solution)/shard_map/ppermute | solution.py:86
  170.1 5.0 %collective-permute-start.10 = (bf16[2,8,384]{2,0,1:T(2,128)(2,1)S(1)}, bf16[2,8,384]{2,0,1:T(2,128)(2,1)S(1)}, u32[]{:S(2)}, u32[]{:S(2)}) collective-permute-start(bf16[2,8,384]{2,0,1:T(2,128)(2,1)S(1)} %copy-done.12), channel_id=1, source_target_pairs={{0,11},{1,10},{2,9},{3,8},{4,15},{5,14},{6,13},{7,12},{8,3},{9,2},... | collective-permute-start | bytes 36872 | tf_op jit(solution)/shard_map/ppermute | solution.py:86
  175.2 4.1 %collective-permute-done.10 = bf16[2,8,384]{2,0,1:T(2,128)(2,1)S(1)} collective-permute-done((bf16[2,8,384]{2,0,1:T(2,128)(2,1)S(1)}, bf16[2,8,384]{2,0,1:T(2,128)(2,1)S(1)}, u32[]{:S(2)}, u32[]{:S(2)}) %collective-permute-start.10) | collective-permute-done | bytes 12320 | tf_op jit(solution)/shard_map/ppermute | solution.py:86
  181.2 4.0 %reshape.455 = bf16[9,16,2,12,24]{3,2,1,4,0:T(2,128)(2,1)S(1)} reshape(bf16[9,384,24]{1,2,0:T(8,128)(2,1)S(1)} %reduce_sum.33) | data formatting | bytes 331776 | tf_op jit(solution)/shard_map/reshape | solution.py:121
  189.0 3.8 %all_to_all.30 = bf16[2,2,20736]{2,1,0:T(2,128)(2,1)S(1)} all-to-all(bf16[2,2,20736]{2,1,0:T(2,128)(2,1)S(1)} %reshape.463), channel_id=1, replica_groups=mesh['z'=16,'c'=2,'freq'=16] {'c'}, dimensions={0} | all-to-all | bytes 331776 | tf_op jit(solution)/shard_map/all_to_all | solution.py:124
  195.6 17.4 %all-to-all-start.3 = ((bf16[16,2,1296]{2,1,0:T(2,128)(2,1)}), bf16[16,2,1296]{2,1,0:T(2,128)(2,1)S(1)}, u32[]{:S(2)}, u32[]{:S(2)}) async-start(bf16[16,2,1296]{2,1,0:T(2,128)(2,1)} %reshape.465), calls=%async_computation.3 | async-start | bytes 180224 | tf_op jit(solution)/shard_map/all_to_all | solution.py:126
  214.5 12.2 %all-to-all-done.3 = bf16[16,2,1296]{2,1,0:T(2,128)(2,1)S(1)} async-done(((bf16[16,2,1296]{2,1,0:T(2,128)(2,1)}), bf16[16,2,1296]{2,1,0:T(2,128)(2,1)S(1)}, u32[]{:S(2)}, u32[]{:S(2)}) %all-to-all-start.3) | async-done | bytes 82976 | tf_op jit(solution)/shard_map/all_to_all | solution.py:126
  (131 shorter events, 69.4 us)
Async XLA Ops:
  7.8 14.7 %all-to-all-start = ((bf16[2,2,128,384]{3,1,0,2:T(2,128)(2,1)}), bf16[2,2,128,384]{3,1,0,2:T(2,128)(2,1)S(1)}, u32[]{:S(2)}, u32[]{:S(2)}) async-start(bf16[2,2,128,384]{3,1,0,2:T(2,128)(2,1)} %copy.152), calls=%async_computation | async-start | bytes 786432 | tf_op jit(solution)/shard_map/all_to_all | solution.py:53
  41.2 172.5 %collective-permute-start.14 = (bf16[2,8,384]{2,0,1:T(2,128)(2,1)S(1)}, bf16[2,8,384]{2,0,1:T(2,128)(2,1)}, u32[]{:S(2)}, u32[]{:S(2)}) collective-permute-start(bf16[2,8,384]{2,0,1:T(2,128)(2,1)S(1)} %get-tuple-element.18), channel_id=1, source_target_pairs={{0,15},{1,14},{2,13},{3,12},{4,11},{5,10},{6,9},{7,8},{8,7},{9,6},... | collective-permute-start | bytes 36872 | tf_op jit(solution)/shard_map/ppermute | solution.py:86
  45.9 167.1 %collective-permute-start.13 = (bf16[2,8,384]{2,0,1:T(2,128)(2,1)}, bf16[2,8,384]{2,0,1:T(2,128)(2,1)}, u32[]{:S(2)}, u32[]{:S(2)}) collective-permute-start(bf16[2,8,384]{2,0,1:T(2,128)(2,1)} %get-tuple-element.19), channel_id=1, source_target_pairs={{0,14},{1,15},{2,12},{3,13},{4,10},{5,11},{6,8},{7,9},{8,6},{9,7},... | collective-permute-start | bytes 36872 | tf_op jit(solution)/shard_map/ppermute | solution.py:86
  49.2 130.8 %collective-permute-start.12 = (bf16[2,8,384]{2,0,1:T(2,128)(2,1)}, bf16[2,8,384]{2,0,1:T(2,128)(2,1)}, u32[]{:S(2)}, u32[]{:S(2)}) collective-permute-start(bf16[2,8,384]{2,0,1:T(2,128)(2,1)} %get-tuple-element.20), channel_id=1, source_target_pairs={{0,13},{1,12},{2,15},{3,14},{4,9},{5,8},{6,11},{7,10},{8,5},{9,4},... | collective-permute-start | bytes 36872 | tf_op jit(solution)/shard_map/ppermute | solution.py:86
  52.5 126.8 %collective-permute-start.11 = (bf16[2,8,384]{2,0,1:T(2,128)(2,1)}, bf16[2,8,384]{2,0,1:T(2,128)(2,1)}, u32[]{:S(2)}, u32[]{:S(2)}) collective-permute-start(bf16[2,8,384]{2,0,1:T(2,128)(2,1)} %get-tuple-element.21), channel_id=1, source_target_pairs={{0,12},{1,13},{2,14},{3,15},{4,8},{5,9},{6,10},{7,11},{8,4},{9,5},... | collective-permute-start | bytes 36872 | tf_op jit(solution)/shard_map/ppermute | solution.py:86
  55.4 28.4 %collective-permute-start = (bf16[2,8,384]{2,0,1:T(2,128)(2,1)}, bf16[2,8,384]{2,0,1:T(2,128)(2,1)}, u32[]{:S(2)}, u32[]{:S(2)}) collective-permute-start(bf16[2,8,384]{2,0,1:T(2,128)(2,1)} %get-tuple-element.32), channel_id=1, source_target_pairs={{0,1},{1,0},{2,3},{3,2},{4,5},{5,4},{6,7},{7,6},{8,9},{9,8},{10,11... | collective-permute-start | bytes 36872 | tf_op jit(solution)/shard_map/ppermute | solution.py:86
  74.6 53.8 %copy-start.17 = (bf16[2,8,384]{2,0,1:T(2,128)(2,1)S(1)}, bf16[2,8,384]{2,0,1:T(2,128)(2,1)}, u32[]{:S(2)}) copy-start(bf16[2,8,384]{2,0,1:T(2,128)(2,1)} %get-tuple-element.27) | copy-start | bytes 36868
  74.6 61.7 %copy-start.16 = (bf16[2,8,384]{2,0,1:T(2,128)(2,1)S(1)}, bf16[2,8,384]{2,0,1:T(2,128)(2,1)}, u32[]{:S(2)}) copy-start(bf16[2,8,384]{2,0,1:T(2,128)(2,1)} %get-tuple-element.26) | copy-start | bytes 36868
  74.6 69.4 %copy-start.15 = (bf16[2,8,384]{2,0,1:T(2,128)(2,1)S(1)}, bf16[2,8,384]{2,0,1:T(2,128)(2,1)}, u32[]{:S(2)}) copy-start(bf16[2,8,384]{2,0,1:T(2,128)(2,1)} %get-tuple-element.25) | copy-start | bytes 36868
  74.7 78.0 %copy-start.14 = (bf16[2,8,384]{2,0,1:T(2,128)(2,1)S(1)}, bf16[2,8,384]{2,0,1:T(2,128)(2,1)}, u32[]{:S(2)}) copy-start(bf16[2,8,384]{2,0,1:T(2,128)(2,1)} %get-tuple-element.24) | copy-start | bytes 36868
  74.7 86.0 %copy-start.13 = (bf16[2,8,384]{2,0,1:T(2,128)(2,1)S(1)}, bf16[2,8,384]{2,0,1:T(2,128)(2,1)}, u32[]{:S(2)}) copy-start(bf16[2,8,384]{2,0,1:T(2,128)(2,1)} %get-tuple-element.23) | copy-start | bytes 36868
  74.7 95.4 %copy-start.12 = (bf16[2,8,384]{2,0,1:T(2,128)(2,1)S(1)}, bf16[2,8,384]{2,0,1:T(2,128)(2,1)}, u32[]{:S(2)}) copy-start(bf16[2,8,384]{2,0,1:T(2,128)(2,1)} %get-tuple-element.22) | copy-start | bytes 36868
  74.7 106.1 %all-to-all-start.1 = ((bf16[16,9,384,24]{2,3,1,0:T(8,128)(2,1)}), bf16[16,9,384,24]{2,3,1,0:T(8,128)(2,1)S(1)}, u32[]{:S(2)}, u32[]{:S(2)}) async-start(bf16[16,9,384,24]{2,3,1,0:T(8,128)(2,1)} %copy.182), calls=%async_computation.1 | async-start | bytes 5308416 | tf_op jit(solution)/shard_map/all_to_all | solution.py:116
  83.8 25.7 %collective-permute-start.1 = (bf16[2,8,384]{2,0,1:T(2,128)(2,1)S(1)}, bf16[2,8,384]{2,0,1:T(2,128)(2,1)S(1)}, u32[]{:S(2)}, u32[]{:S(2)}) collective-permute-start(bf16[2,8,384]{2,0,1:T(2,128)(2,1)S(1)} %copy-done.21), channel_id=1, source_target_pairs={{0,2},{1,3},{2,0},{3,1},{4,6},{5,7},{6,4},{7,5},{8,10},{9,11},{10,... | collective-permute-start | bytes 36872 | tf_op jit(solution)/shard_map/ppermute | solution.py:86
  109.5 6.8 %collective-permute-start.2 = (bf16[2,8,384]{2,0,1:T(2,128)(2,1)S(1)}, bf16[2,8,384]{2,0,1:T(2,128)(2,1)S(1)}, u32[]{:S(2)}, u32[]{:S(2)}) collective-permute-start(bf16[2,8,384]{2,0,1:T(2,128)(2,1)S(1)} %copy-done.20), channel_id=1, source_target_pairs={{0,3},{1,2},{2,1},{3,0},{4,7},{5,6},{6,5},{7,4},{8,11},{9,10},{10,... | collective-permute-start | bytes 36872 | tf_op jit(solution)/shard_map/ppermute | solution.py:86
  116.3 5.6 %collective-permute-start.3 = (bf16[2,8,384]{2,0,1:T(2,128)(2,1)S(1)}, bf16[2,8,384]{2,0,1:T(2,128)(2,1)S(1)}, u32[]{:S(2)}, u32[]{:S(2)}) collective-permute-start(bf16[2,8,384]{2,0,1:T(2,128)(2,1)S(1)} %copy-done.19), channel_id=1, source_target_pairs={{0,4},{1,5},{2,6},{3,7},{4,0},{5,1},{6,2},{7,3},{8,12},{9,13},{10,... | collective-permute-start | bytes 36872 | tf_op jit(solution)/shard_map/ppermute | solution.py:86
  121.9 6.5 %collective-permute-start.4 = (bf16[2,8,384]{2,0,1:T(2,128)(2,1)S(1)}, bf16[2,8,384]{2,0,1:T(2,128)(2,1)S(1)}, u32[]{:S(2)}, u32[]{:S(2)}) collective-permute-start(bf16[2,8,384]{2,0,1:T(2,128)(2,1)S(1)} %copy-done.18), channel_id=1, source_target_pairs={{0,5},{1,4},{2,7},{3,6},{4,1},{5,0},{6,3},{7,2},{8,13},{9,12},{10,... | collective-permute-start | bytes 36872 | tf_op jit(solution)/shard_map/ppermute | solution.py:86
  128.4 8.0 %collective-permute-start.5 = (bf16[2,8,384]{2,0,1:T(2,128)(2,1)S(1)}, bf16[2,8,384]{2,0,1:T(2,128)(2,1)S(1)}, u32[]{:S(2)}, u32[]{:S(2)}) collective-permute-start(bf16[2,8,384]{2,0,1:T(2,128)(2,1)S(1)} %copy-done.17), channel_id=1, source_target_pairs={{0,6},{1,7},{2,4},{3,5},{4,2},{5,3},{6,0},{7,1},{8,14},{9,15},{10,... | collective-permute-start | bytes 36872 | tf_op jit(solution)/shard_map/ppermute | solution.py:86
  136.4 7.7 %collective-permute-start.6 = (bf16[2,8,384]{2,0,1:T(2,128)(2,1)S(1)}, bf16[2,8,384]{2,0,1:T(2,128)(2,1)S(1)}, u32[]{:S(2)}, u32[]{:S(2)}) collective-permute-start(bf16[2,8,384]{2,0,1:T(2,128)(2,1)S(1)} %copy-done.16), channel_id=1, source_target_pairs={{0,7},{1,6},{2,5},{3,4},{4,3},{5,2},{6,1},{7,0},{8,15},{9,14},{10,... | collective-permute-start | bytes 36872 | tf_op jit(solution)/shard_map/ppermute | solution.py:86
  144.1 8.6 %collective-permute-start.7 = (bf16[2,8,384]{2,0,1:T(2,128)(2,1)S(1)}, bf16[2,8,384]{2,0,1:T(2,128)(2,1)S(1)}, u32[]{:S(2)}, u32[]{:S(2)}) collective-permute-start(bf16[2,8,384]{2,0,1:T(2,128)(2,1)S(1)} %copy-done.15), channel_id=1, source_target_pairs={{0,8},{1,9},{2,10},{3,11},{4,12},{5,13},{6,14},{7,15},{8,0},{9,1},... | collective-permute-start | bytes 36872 | tf_op jit(solution)/shard_map/ppermute | solution.py:86
  152.6 8.0 %collective-permute-start.8 = (bf16[2,8,384]{2,0,1:T(2,128)(2,1)S(1)}, bf16[2,8,384]{2,0,1:T(2,128)(2,1)S(1)}, u32[]{:S(2)}, u32[]{:S(2)}) collective-permute-start(bf16[2,8,384]{2,0,1:T(2,128)(2,1)S(1)} %copy-done.14), channel_id=1, source_target_pairs={{0,9},{1,8},{2,11},{3,10},{4,13},{5,12},{6,15},{7,14},{8,1},{9,0},... | collective-permute-start | bytes 36872 | tf_op jit(solution)/shard_map/ppermute | solution.py:86
  160.6 9.5 %collective-permute-start.9 = (bf16[2,8,384]{2,0,1:T(2,128)(2,1)S(1)}, bf16[2,8,384]{2,0,1:T(2,128)(2,1)S(1)}, u32[]{:S(2)}, u32[]{:S(2)}) collective-permute-start(bf16[2,8,384]{2,0,1:T(2,128)(2,1)S(1)} %copy-done.13), channel_id=1, source_target_pairs={{0,10},{1,11},{2,8},{3,9},{4,14},{5,15},{6,12},{7,13},{8,2},{9,3},... | collective-permute-start | bytes 36872 | tf_op jit(solution)/shard_map/ppermute | solution.py:86
  170.1 9.2 %collective-permute-start.10 = (bf16[2,8,384]{2,0,1:T(2,128)(2,1)S(1)}, bf16[2,8,384]{2,0,1:T(2,128)(2,1)S(1)}, u32[]{:S(2)}, u32[]{:S(2)}) collective-permute-start(bf16[2,8,384]{2,0,1:T(2,128)(2,1)S(1)} %copy-done.12), channel_id=1, source_target_pairs={{0,11},{1,10},{2,9},{3,8},{4,15},{5,14},{6,13},{7,12},{8,3},{9,2},... | collective-permute-start | bytes 36872 | tf_op jit(solution)/shard_map/ppermute | solution.py:86
  195.6 31.1 %all-to-all-start.3 = ((bf16[16,2,1296]{2,1,0:T(2,128)(2,1)}), bf16[16,2,1296]{2,1,0:T(2,128)(2,1)S(1)}, u32[]{:S(2)}, u32[]{:S(2)}) async-start(bf16[16,2,1296]{2,1,0:T(2,128)(2,1)} %reshape.465), calls=%async_computation.3 | async-start | bytes 180224 | tf_op jit(solution)/shard_map/all_to_all | solution.py:126
  (18 other events, 224.3 us)
